TPU v7x, 32 devices: a whole 2x2x4 slice. The times are simulated.
32 devices in a mesh: dp: 8 (over z, core), leaf: 4 (over y, x).
Axes of the slice: x: 2, y: 2, z: 4, core: 2. Of those that a mesh axis runs over, the one named last changes fastest.
Arguments:
- features: bfloat16 [51200, 384], P(('dp', 'leaf')), may hold values from -6 to 6
- head_weight: bfloat16 [384, 1536], replicated, may hold values from -0.3125 to 0.3125
- gain: float32 [1536], replicated, may hold values from 0.5 to 1.5
- shift: float32 [1536], replicated, may hold values from -3 to 3
- node_weights: bfloat16 [4096, 1536], P('leaf'), may hold values from -0.15625 to 0.15625
- subtree_map: int32 [64], replicated, may hold values from 0 to 63, each once
- node_ids: int32 [512, 64], P('dp'), may hold values from -1 to 4095, as said below
Outputs:
- head_grad: float32 [384, 1536], P(None, 'dp')
- gain_grad: float32 [1536], P('dp')
- shift_grad: float32 [1536], P('dp')
- node_grad: float32 [4096, 1536], P('leaf', 'dp')
Inputs may be any that keep to these rules, and one draw needn't show every extreme that they name: `node_ids`: each image has 1 to 16 positive ids, all in one subtree, in its first columns, then -1; and 1 to 48 hard-negative ids in another subtree from column 16 on, then -1. Ids of one image are distinct. The first image has full counts.
All inputs are finite; a program needn't handle non-finite values.
Results may differ from a plain program's by a relative error of at most 0.0036.
Values may be sent and summed in bfloat16 or wider, within the bound.
No kernel may reach another device: no remote copies, remote signals or barrier semaphores. Data moves between devices by JAX's collectives and lax.ppermute only.
A program may use at most 128 MiB of HBM per device.

v0:
```python
import jax
import jax.numpy as jnp
from jax import lax
from jax.sharding import PartitionSpec as P

P_SIZE = 100
SUB_SIZE = 64
KPOS = 16


def slot_table(slot_rows, owned_rows, values_rows, slots_dev):
    column = jnp.arange(slots_dev, dtype=jnp.int32)[None, None, :]
    match = (slot_rows[:, :, None] == column) & owned_rows[:, :, None]
    return jnp.sum(jnp.where(match, values_rows[:, :, None], 0.0), axis=1)


def shards(features, head_weight, gain, shift, node_weights, subtree_map, node_ids):
    images_here = features.shape[0] // P_SIZE
    width = head_weight.shape[1]
    linear_scores = jnp.dot(features, head_weight, preferred_element_type=jnp.float32)
    shifted = gain * linear_scores + shift
    sig = jax.nn.sigmoid(shifted)
    active = shifted * sig
    embedded = jnp.mean(active.reshape(images_here, P_SIZE, width), axis=1).astype(jnp.bfloat16)
    grouped = lax.all_gather(embedded, "leaf", axis=0, tiled=True)
    slots_dev = node_weights.shape[0]
    valid_pair = node_ids >= 0
    safe_ids = jnp.where(valid_pair, node_ids, 0)
    subtree = safe_ids // SUB_SIZE
    matches = (
        subtree[:, :, None] == jnp.arange(subtree_map.shape[0], dtype=jnp.int32)[None, None, :]
    )
    placed = jnp.sum(jnp.where(matches, subtree_map[None, None, :], 0), axis=2)
    slot_row = placed * SUB_SIZE + safe_ids % SUB_SIZE
    owned = valid_pair & (slot_row // slots_dev == lax.axis_index("leaf"))
    local_slot = jnp.where(owned, slot_row % slots_dev, 0)
    scores = lax.dot_general(
        grouped, node_weights, (((1,), (1,)), ((), ())), preferred_element_type=jnp.float32
    )
    target = (jnp.arange(node_ids.shape[1]) < KPOS).astype(jnp.float32)
    hit_count = slot_table(local_slot, owned, jnp.ones(local_slot.shape, jnp.float32), slots_dev)
    positive = slot_table(
        local_slot, owned, jnp.broadcast_to(target[None, :], local_slot.shape), slots_dev
    )
    table = jnp.where(hit_count > 0.5, jax.nn.sigmoid(scores) - positive, 0.0).astype(jnp.bfloat16)
    grad_part = jnp.dot(table, node_weights, preferred_element_type=jnp.float32)
    emb_grad = lax.psum_scatter(grad_part, "leaf", scatter_dimension=0, tiled=True)
    column_ids = jnp.arange(slots_dev, dtype=jnp.int32)[None, None, :]
    pick = (local_slot[:, :, None] == column_ids) & owned[:, :, None]
    coef = jnp.sum(jnp.where(pick, table.astype(jnp.float32)[:, None, :], 0.0), axis=2).astype(
        jnp.bfloat16
    )
    columns = lax.all_to_all(grouped, "dp", split_axis=1, concat_axis=0, tiled=True)
    all_coef = lax.all_gather(coef, "dp", axis=0, tiled=True)
    all_slot = lax.all_gather(local_slot, "dp", axis=0, tiled=True)
    every_pair = jnp.ones(all_slot.shape, jnp.bool_)
    all_table = slot_table(all_slot, every_pair, all_coef.astype(jnp.float32), slots_dev).astype(
        jnp.bfloat16
    )
    node_grad = lax.dot_general(
        all_table, columns, (((0,), (0,)), ((), ())), preferred_element_type=jnp.float32
    )
    slope = (sig * (1.0 + shifted * (1.0 - sig))).reshape(images_here, P_SIZE, width)
    pixel_gradient = ((emb_grad / P_SIZE)[:, None, :] * slope).reshape(images_here * P_SIZE, width)
    lin_grad = (pixel_gradient * gain).astype(jnp.bfloat16)
    head_term = lax.dot_general(
        features, lin_grad, (((0,), (0,)), ((), ())), preferred_element_type=jnp.float32
    )
    gain_term = jnp.sum(pixel_gradient * linear_scores, axis=0)
    shift_term = jnp.sum(pixel_gradient, axis=0)
    split_sums = (
        lax.psum_scatter(head_term, "dp", scatter_dimension=1, tiled=True),
        lax.psum_scatter(gain_term, "dp", scatter_dimension=0, tiled=True),
        lax.psum_scatter(shift_term, "dp", scatter_dimension=0, tiled=True),
    )
    head_grad, gain_grad, shift_grad = lax.psum(
        (split_sums[0], split_sums[1], split_sums[2]), "leaf"
    )
    return (head_grad, gain_grad, shift_grad, node_grad)


def solution(mesh):
    in_specs = (P(("dp", "leaf"), None), P(), P(), P(), P("leaf", None), P(), P("dp", None))
    out_specs = (P(None, "dp"), P("dp"), P("dp"), P("leaf", "dp"))
    return jax.shard_map(shards, mesh=mesh, in_specs=in_specs, out_specs=out_specs, check_vma=False)
```

profile of v0, /device:TPU:0, one launch (start us, length us, event | category | flops | bytes accessed | tf_op | source)
XLA Modules:
  0.0 237.6 jit_solution(990321862324019750)
XLA Ops:
  7.2 0.0 copy-start
  7.2 0.0 reduce-scatter.3.cloned.1.call-start
  7.2 0.9 add_select_fusion.3
  8.2 11.9 %fusion.1 = (f32[1600,1536]{1,0:T(8,128)}, f32[1600,1536]{1,0:T(8,128)}) fusion(f32[1536]{0:T(1024)} %param.10, f32[1536]{0:T(1024)} %param.9, bf16[1600,384]{1,0:T(8,128)(2,1)} %param.7, bf16[384,1536]{1,0:T(8,128)(2,1)} %param.8), kind=kOutput, calls=%fused_computation.11 | convolution fusion | flops 1902182400 | bytes 22081536 | tf_op jit(solution)/shard_map/dot_general | solution.py:20
  20.1 10.0 %reshape.27 = f32[16,100,1536]{2,1,0:T(8,128)} reshape(f32[1600,1536]{1,0:T(8,128)} %get-tuple-element.15) | data formatting | bytes 19660800 | tf_op jit(solution)/shard_map/reshape | solution.py:24
  30.1 0.0 copy-start.4
  30.1 0.0 copy-start.1
  30.1 5.3 %reduce_sum.74 = f32[16,1536]{1,0:T(8,128)S(1)} reduce(f32[16,100,1536]{2,1,0:T(8,128)} %reshape.27, f32[]{:T(128)} %constant.65.clone.1), dimensions={1}, to_apply=%region_2.3 | reduce | flops 2433024 | bytes 9928708 | tf_op jit(solution)/shard_map/reduce_sum | solution.py:24
  35.5 10.2 %all_gather.9 = bf16[64,1536]{1,0:T(8,128)(2,1)S(1)} all-gather(bf16[16,1536]{1,0:T(8,128)(2,1)S(1)} %multiply_convert_fusion.4), channel_id=1, replica_groups=mesh['dp'=8,'leaf'=4] {'leaf'}, dimensions={0}, use_global_device_ids=true | all-gather | bytes 245760 | tf_op jit(solution)/shard_map/all_gather | solution.py:25
  45.6 0.0 copy-done.4
  45.6 1.8 select_reduce_fusion.4
  47.5 0.0 copy-done.1
  47.5 0.1 fusion.15
  47.6 9.4 %select_reduce_fusion.3 = (f32[64,1024]{1,0:T(8,128)S(1)}, f32[64,1024]{1,0:T(8,128)S(1)}) fusion(s32[64,64]{1,0:T(8,128)S(1)} %get-tuple-element.13, pred[64,64]{1,0:T(8,128)(4,1)S(1)} %get-tuple-element.14, f32[64]{0:T(128)S(1)} %compare_convert_fusion), kind=kLoop, calls=%fused_computation.4 | loop fusion | flops 25034752 | bytes 545024 | tf_op jit(solution)/shard_map/reduce_sum | solution.py:14
  56.9 0.0 copy-done
  56.9 1.8 fusion.21
  58.7 1.4 fusion.22
  60.1 0.0 reduce-scatter.3.cloned.1.call-update
  60.2 0.2 reduce-scatter.5.cloned.1.call-start
  60.4 24.7 %reduce-scatter.3.cloned.1.call-done = f32[16,1536]{1,0:T(8,128)} async-done(((f32[64,1536]{1,0:T(8,128)}), f32[16,1536]{1,0:T(8,128)}) %reduce-scatter.3.cloned.1.call-update) | async-done | bytes 98320 | tf_op jit(solution)/shard_map/reduce_scatter | solution.py:47
  85.1 0.9 broadcast_multiply_fusion
  86.0 5.2 %mul.45 = f32[16,100,1536]{2,1,0:T(8,128)} broadcast(f32[16,1536]{1,0:T(8,128)S(1)} %broadcast_multiply_fusion), dimensions={0,2} | broadcast | bytes 9928704 | tf_op jit(solution)/shard_map/mul | solution.py:64
  91.1 0.0 copy-start.2
  91.2 0.0 copy-start.3
  91.2 10.0 %mul.46 = f32[1600,1536]{1,0:T(8,128)} reshape(f32[16,100,1536]{2,1,0:T(8,128)} %mul.45) | data formatting | bytes 19660800 | tf_op jit(solution)/shard_map/mul | solution.py:64
  101.2 0.0 copy-done.2
  101.2 0.0 copy-done.3
  101.2 0.0 copy-start.5
  101.2 9.0 %fusion.20 = (f32[1536]{0:T(1024)S(1)}, f32[1536]{0:T(1024)S(1)}, f32[1600,1536]{1,0:T(8,128)S(1)}) fusion(f32[1600,1536]{1,0:T(8,128)} %get-tuple-element.16, f32[1600,1536]{1,0:T(8,128)} %mul.46, f32[1536]{0:T(1024)S(1)} %copy-done.2, f32[1536]{0:T(1024)S(1)} %copy-done.3), kind=kLoop, calls=%fused_computation.52 | loop fusion | flops 31945728 | bytes 29515776 | tf_op jit(solution)/shard_map/reduce_sum | solution.py:70
  110.2 0.0 copy-done.5
  110.3 0.0 copy-start.6
  110.3 4.5 %fusion.4 = f32[384,1536]{0,1:T(8,128)} fusion(bf16[1600,384]{1,0:T(8,128)(2,1)S(1)} %copy-done.5, f32[1600,1536]{1,0:T(8,128)S(1)} %get-tuple-element.12, f32[1536]{0:T(1024)S(1)} %copy-done.3), kind=kOutput, calls=%fused_computation.15 | convolution fusion | flops 1892352000 | bytes 13424640 | tf_op jit(solution)/shard_map/dot_general | solution.py:66
  114.7 0.0 reduce-scatter.5.cloned.1.call-update
  114.8 0.9 all_to_all.14
  115.7 1.7 copy.13
  117.4 4.6 %all-to-all-start = ((bf16[64,8,192]{2,0,1:T(8,128)(2,1)}), bf16[64,8,192]{2,0,1:T(8,128)(2,1)}, u32[]{:S(2)}, u32[]{:S(2)}) async-start(bf16[64,8,192]{2,0,1:T(8,128)(2,1)} %copy.13), calls=%async_computation.2 | async-start | bytes 524288 | tf_op jit(solution)/shard_map/all_to_all | solution.py:53
  122.0 0.0 all-reduce.6.cloned.1.call-start
  122.1 5.3 %select_reduce_fusion.1 = bf16[64,64]{1,0:T(8,128)(2,1)S(1)} fusion(f32[64,1024]{1,0:T(8,128)} %get-tuple-element.17, s32[64,64]{1,0:T(8,128)S(1)} %get-tuple-element.13, pred[64,64]{1,0:T(8,128)(4,1)S(1)} %get-tuple-element.14), kind=kLoop, calls=%fused_computation.2 | loop fusion | flops 16773120 | bytes 290816 | tf_op jit(solution)/shard_map/reduce_sum | solution.py:50
  127.4 16.8 %all_gather.11 = bf16[512,64]{1,0:T(8,128)(2,1)S(1)} all-gather(bf16[64,64]{1,0:T(8,128)(2,1)S(1)} %select_reduce_fusion.1), channel_id=1, replica_groups=mesh['dp'=8,'leaf'=4] {'dp'}, dimensions={0}, use_global_device_ids=true | all-gather | bytes 73728 | tf_op jit(solution)/shard_map/all_gather | solution.py:54
  144.3 15.8 %all_gather.10 = s32[512,64]{1,0:T(8,128)} all-gather(s32[64,64]{1,0:T(8,128)S(1)} %get-tuple-element.13), channel_id=1, replica_groups=mesh['dp'=8,'leaf'=4] {'dp'}, dimensions={0}, use_global_device_ids=true | all-gather | bytes 147456 | tf_op jit(solution)/shard_map/all_gather | solution.py:55
  160.1 0.0 reduce-scatter.5.cloned.1.call-done
  160.1 0.0 all-reduce.6.cloned.1.call-update
  160.1 28.2 %select_reduce_fusion = bf16[512,1024]{1,0:T(8,128)(2,1)} fusion(f32[512,64]{1,0:T(8,128)S(1)} %convert_element_type.30, s32[512,64]{1,0:T(8,128)} %all_gather.10), kind=kLoop, calls=%fused_computation | loop fusion | flops 100139008 | bytes 1310720 | tf_op jit(solution)/shard_map/reduce_sum | solution.py:14
  188.3 0.0 copy-done.6
  188.3 0.6 dynamic-slice
  189.6 0.0 all-to-all-done
  189.6 2.6 %fusion.23 = f32[1024,192]{0,1:T(8,128)} fusion(bf16[512,1024]{1,0:T(8,128)(2,1)} %select_reduce_fusion, bf16[512,192]{1,0:T(8,128)(2,1)} %bitcast.2), kind=kOutput, calls=%fused_computation.55 | convolution fusion | flops 201326592 | bytes 2031616 | tf_op jit(solution)/shard_map/dot_general | solution.py:60
  192.1 27.6 %all-reduce.2 = (f32[1536]{0:T(1024)S(1)}, f32[1536]{0:T(1024)S(1)}) all-reduce(f32[1536]{0:T(1024)S(1)} %get-tuple-element.5, f32[1536]{0:T(1024)S(1)} %get-tuple-element.4), channel_id=4, replica_groups=mesh['dp'=8,'leaf'=4] {'dp'}, use_global_device_ids=true, to_apply=%region_8.9.clone | all-reduce | flops 3072 | bytes 24576
  219.8 0.1 dynamic-slice.1
  219.8 0.1 dynamic-slice.3
  219.9 9.4 %all-reduce.3 = (f32[192]{0:T(256)}, f32[192]{0:T(256)}) all-reduce(f32[192]{0:T(256)S(1)} %dynamic-slice.1, f32[192]{0:T(256)S(1)} %dynamic-slice.3), channel_id=1, replica_groups=mesh['dp'=8,'leaf'=4] {'leaf'}, use_global_device_ids=true, to_apply=%region_9.10 | all-reduce | flops 384 | bytes 3072 | tf_op jit(solution)/shard_map/psum | solution.py:76
  229.4 0.0 all-reduce.6.cloned.1.call-done
  229.4 1.7 copy.15
  (3 shorter events, 0.0 us)
Async XLA Ops:
  7.2 49.8 %copy-start = (bf16[1024,1536]{1,0:T(8,128)(2,1)S(1)}, bf16[1024,1536]{1,0:T(8,128)(2,1)}, u32[]{:S(2)}) copy-start(bf16[1024,1536]{1,0:T(8,128)(2,1)} %param.11) | copy-start | bytes 9437188
  7.2 77.9 %reduce-scatter.3.cloned.1.call-start = ((), (), s32[]{:S(2)}) async-start(), calls=%async_computation.3 | async-start | bytes 491520 | tf_op jit(solution)/shard_map/reduce_scatter | solution.py:47
  30.1 15.5 %copy-start.4 = (s32[64]{0:T(128)S(1)}, s32[64]{0:T(128)}, u32[]{:S(2)}) copy-start(s32[64]{0:T(128)} %param.12) | copy-start | bytes 772
  30.1 17.3 %copy-start.1 = (s32[64,64]{1,0:T(8,128)S(1)}, s32[64,64]{1,0:T(8,128)}, u32[]{:S(2)}) copy-start(s32[64,64]{1,0:T(8,128)} %param.13) | copy-start | bytes 49156
  60.2 99.9 %reduce-scatter.5.cloned.1.call-start = ((), (), s32[]{:S(2)}) async-start(), calls=%async_computation.4 | async-start | bytes 2654208 | tf_op jit(solution)/shard_map/reduce_scatter | solution.py:72
  91.1 10.1 %copy-start.2 = (f32[1536]{0:T(1024)S(1)}, f32[1536]{0:T(1024)}, u32[]{:S(2)}) copy-start(f32[1536]{0:T(1024)} %param.10) | copy-start | bytes 18436
  91.2 10.1 %copy-start.3 = (f32[1536]{0:T(1024)S(1)}, f32[1536]{0:T(1024)}, u32[]{:S(2)}) copy-start(f32[1536]{0:T(1024)} %param.9) | copy-start | bytes 18436
  101.2 9.0 %copy-start.5 = (bf16[1600,384]{1,0:T(8,128)(2,1)S(1)}, bf16[1600,384]{1,0:T(8,128)(2,1)}, u32[]{:S(2)}) copy-start(bf16[1600,384]{1,0:T(8,128)(2,1)} %param.7) | copy-start | bytes 3686404
  110.3 78.1 %copy-start.6 = (u32[32]{0:T(128)S(1)}, u32[32]{0:T(128)}, u32[]{:S(2)}) copy-start(u32[32]{0:T(128)} %constant.71) | copy-start | bytes 388
  117.4 72.2 %all-to-all-start = ((bf16[64,8,192]{2,0,1:T(8,128)(2,1)}), bf16[64,8,192]{2,0,1:T(8,128)(2,1)}, u32[]{:S(2)}, u32[]{:S(2)}) async-start(bf16[64,8,192]{2,0,1:T(8,128)(2,1)} %copy.13), calls=%async_computation.2 | async-start | bytes 524288 | tf_op jit(solution)/shard_map/all_to_all | solution.py:53
  122.0 107.4 %all-reduce.6.cloned.1.call-start = ((), (), s32[]{:S(2)}) async-start(), calls=%async_computation.5 | async-start | bytes 589824 | tf_op jit(solution)/shard_map/psum | solution.py:76
Sparse Core Ops, SparseCore 0:
  60.3 24.7 reduce-scatter.2
  114.9 41.0 reduce-scatter.4
  160.2 41.8 all-reduce.5
where the time goes:
time: 239 us; the launch traced here: 238 us
  blocking collectives  79.9 us (33%)
  other arithmetic  61 us (26%)
  local copies, waits for them, and re-layouts  30.4 us (13%)
  waiting for transfers between devices  24.7 us (10%)
  matrix products  22.2 us (9%)
  between operations  14.5 us (6%)
  starting transfers between devices  4.89 us (2%)
    reduce_sum x2, other arithmetic, slot_table(): return jnp.sum(jnp.where(match, values_rows[:, :, None], 0.0), axis=1)  37.6 us
    unnamed x1, blocking collectives  27.6 us
    reduce_scatter x1, waiting for transfers between devices, shards(): lax.psum_scatter(grad_part, 'leaf', scatter_dimension=0, tiled=True)  24.7 us
    all_gather x1, blocking collectives, shards(): all_coef = lax.all_gather(coef, 'dp', axis=0, tiled=True)  16.8 us
    all_gather x1, blocking collectives, shards(): all_slot = lax.all_gather(local_slot, 'dp', axis=0, tiled=True)  15.8 us
    mul x2, local copies, waits for them, and re-layouts, shards(): (emb_grad / P_SIZE)[:, None, :] * slope  15.2 us
    dot_general x1, matrix products, shards(): jnp.dot(features, head_weight, preferred_element_type=jnp.float32)  11.9 us
    all_gather x1, blocking collectives, shards(): grouped = lax.all_gather(embedded, 'leaf', axis=0, tiled=True)  10.2 us
  transfers between devices with their start and end apart: 4, of which 1 were waited for; matrix products, arithmetic and copies ran while one was open for 16% of the time, Pallas kernels for 0%

commit v1 on v0

--- a/solution.py
+++ b/solution.py
@@ -51,7 +51,12 @@
         jnp.bfloat16
     )
     columns = lax.all_to_all(grouped, "dp", split_axis=1, concat_axis=0, tiled=True)
-    all_coef = lax.all_gather(coef, "dp", axis=0, tiled=True)
+    ring = [coef]
+    for hop in range(7):
+        ring.append(lax.ppermute(ring[-1], "dp", [(dev, (dev + 1) % 8) for dev in range(8)]))
+    all_coef = jnp.roll(
+        jnp.concatenate(ring[::-1], axis=0), (lax.axis_index("dp") + 1) * ring[0].shape[0], axis=0
+    )
     all_slot = lax.all_gather(local_slot, "dp", axis=0, tiled=True)
     every_pair = jnp.ones(all_slot.shape, jnp.bool_)
     all_table = slot_table(all_slot, every_pair, all_coef.astype(jnp.float32), slots_dev).astype(

time: 239 us -> 253 us (1.059)
  waiting for transfers between devices: 24.7 us -> 50.6 us
  blocking collectives: 79.9 us -> 64.3 us
    ppermute x0 -> x7, waiting for transfers between devices: none -> 25.9 us  [shards(): lax.ppermute(ring[-1], 'dp', [(dev, (dev + 1) % 8) for dev in range(8)])]
    all_gather x1 -> x0, blocking collectives: 16.8 us -> none  [shards(): all_coef = lax.all_gather(coef, 'dp', axis=0, tiled=True)]
  transfers between devices with their start and end apart: 4 -> 11, of which waited for: 1 -> 6; matrix products, arithmetic and copies ran while one was open for 16% -> 16% of each run, Pallas kernels for 0% -> 0%
where the time goes in v1:
time: 253 us; the launch traced here: 252 us
  blocking collectives  64.3 us (25%)
  other arithmetic  62.4 us (25%)
  waiting for transfers between devices  50.6 us (20%)
  local copies, waits for them, and re-layouts  32.6 us (13%)
  matrix products  22.2 us (9%)
  between operations  14.6 us (6%)
  starting transfers between devices  5.68 us (2%)
    reduce_sum x2, other arithmetic, slot_table(): return jnp.sum(jnp.where(match, values_rows[:, :, None], 0.0), axis=1)  37.6 us
    unnamed x1, blocking collectives  26.9 us
    ppermute x7, waiting for transfers between devices, shards(): lax.ppermute(ring[-1], 'dp', [(dev, (dev + 1) % 8) for dev in range(8)])  25.9 us
    reduce_scatter x1, waiting for transfers between devices, shards(): lax.psum_scatter(grad_part, 'leaf', scatter_dimension=0, tiled=True)  24.7 us
    all_gather x1, blocking collectives, shards(): all_slot = lax.all_gather(local_slot, 'dp', axis=0, tiled=True)  17.5 us
    mul x2, local copies, waits for them, and re-layouts, shards(): (emb_grad / P_SIZE)[:, None, :] * slope  15.2 us
    dot_general x1, matrix products, shards(): jnp.dot(features, head_weight, preferred_element_type=jnp.float32)  11.9 us
    all_gather x1, blocking collectives, shards(): grouped = lax.all_gather(embedded, 'leaf', axis=0, tiled=True)  10.2 us
  transfers between devices with their start and end apart: 11, of which 6 were waited for; matrix products, arithmetic and copies ran while one was open for 16% of the time, Pallas kernels for 0%

profile of v1, /device:TPU:0, one launch (start us, length us, event | category | flops | bytes accessed | tf_op | source)
XLA Modules:
  0.0 252.2 jit_solution(6073692515959603875)
XLA Ops:
  7.2 0.0 copy-start
  7.2 0.0 reduce-scatter.3.cloned.1.call-start
  7.2 0.9 add_select_fusion.3
  8.2 11.9 %fusion.1 = (f32[1600,1536]{1,0:T(8,128)}, f32[1600,1536]{1,0:T(8,128)}) fusion(f32[1536]{0:T(1024)} %param.10, f32[1536]{0:T(1024)} %param.9, bf16[1600,384]{1,0:T(8,128)(2,1)} %param.7, bf16[384,1536]{1,0:T(8,128)(2,1)} %param.8), kind=kOutput, calls=%fused_computation.11 | convolution fusion | flops 1902182400 | bytes 22081536 | tf_op jit(solution)/shard_map/dot_general | solution.py:20
  20.1 10.0 %reshape.27 = f32[16,100,1536]{2,1,0:T(8,128)} reshape(f32[1600,1536]{1,0:T(8,128)} %get-tuple-element.15) | data formatting | bytes 19660800 | tf_op jit(solution)/shard_map/reshape | solution.py:24
  30.1 0.0 copy-start.4
  30.1 0.0 copy-start.1
  30.1 5.3 %reduce_sum.74 = f32[16,1536]{1,0:T(8,128)S(1)} reduce(f32[16,100,1536]{2,1,0:T(8,128)} %reshape.27, f32[]{:T(128)} %constant.87.clone.1), dimensions={1}, to_apply=%region_2.3 | reduce | flops 2433024 | bytes 9928708 | tf_op jit(solution)/shard_map/reduce_sum | solution.py:24
  35.5 10.2 %all_gather.6 = bf16[64,1536]{1,0:T(8,128)(2,1)S(1)} all-gather(bf16[16,1536]{1,0:T(8,128)(2,1)S(1)} %multiply_convert_fusion.4), channel_id=1, replica_groups=mesh['dp'=8,'leaf'=4] {'leaf'}, dimensions={0}, use_global_device_ids=true | all-gather | bytes 245760 | tf_op jit(solution)/shard_map/all_gather | solution.py:25
  45.6 0.0 copy-done.4
  45.6 1.8 select_reduce_fusion.4
  47.5 0.0 copy-done.1
  47.5 0.1 fusion.15
  47.6 9.4 %select_reduce_fusion.3 = (f32[64,1024]{1,0:T(8,128)S(1)}, f32[64,1024]{1,0:T(8,128)S(1)}) fusion(s32[64,64]{1,0:T(8,128)S(1)} %get-tuple-element.13, pred[64,64]{1,0:T(8,128)(4,1)S(1)} %get-tuple-element.14, f32[64]{0:T(128)S(1)} %compare_convert_fusion), kind=kLoop, calls=%fused_computation.4 | loop fusion | flops 25034752 | bytes 545024 | tf_op jit(solution)/shard_map/reduce_sum | solution.py:14
  56.9 0.0 copy-done
  56.9 1.8 fusion.21
  58.7 1.4 fusion.22
  60.1 0.0 reduce-scatter.3.cloned.1.call-update
  60.2 0.2 reduce-scatter.5.cloned.1.call-start
  60.4 24.7 %reduce-scatter.3.cloned.1.call-done = f32[16,1536]{1,0:T(8,128)} async-done(((f32[64,1536]{1,0:T(8,128)}), f32[16,1536]{1,0:T(8,128)}) %reduce-scatter.3.cloned.1.call-update) | async-done | bytes 98320 | tf_op jit(solution)/shard_map/reduce_scatter | solution.py:47
  85.1 0.9 broadcast_multiply_fusion
  86.0 5.2 %mul.48 = f32[16,100,1536]{2,1,0:T(8,128)} broadcast(f32[16,1536]{1,0:T(8,128)S(1)} %broadcast_multiply_fusion), dimensions={0,2} | broadcast | bytes 9928704 | tf_op jit(solution)/shard_map/mul | solution.py:69
  91.1 0.0 copy-start.2
  91.2 0.0 copy-start.3
  91.2 10.0 %mul.49 = f32[1600,1536]{1,0:T(8,128)} reshape(f32[16,100,1536]{2,1,0:T(8,128)} %mul.48) | data formatting | bytes 19660800 | tf_op jit(solution)/shard_map/mul | solution.py:69
  101.2 0.0 copy-done.2
  101.2 0.0 copy-done.3
  101.2 9.6 %fusion.20 = (f32[1536]{0:T(1024)}, f32[1536]{0:T(1024)}, f32[1600,1536]{1,0:T(8,128)S(1)}) fusion(f32[1600,1536]{1,0:T(8,128)} %get-tuple-element.16, f32[1600,1536]{1,0:T(8,128)} %mul.49, f32[1536]{0:T(1024)S(1)} %copy-done.2, f32[1536]{0:T(1024)S(1)} %copy-done.3), kind=kLoop, calls=%fused_computation.69 | loop fusion | flops 31945728 | bytes 29515776 | tf_op jit(solution)/shard_map/reduce_sum | solution.py:75
  110.8 0.0 copy-done.5
  110.8 4.5 %fusion.4 = f32[384,1536]{0,1:T(8,128)} fusion(bf16[1600,384]{1,0:T(8,128)(2,1)S(1)} %copy-done.5, f32[1600,1536]{1,0:T(8,128)S(1)} %get-tuple-element.12, f32[1536]{0:T(1024)S(1)} %copy-done.3), kind=kOutput, calls=%fused_computation.15 | convolution fusion | flops 1892352000 | bytes 13424640 | tf_op jit(solution)/shard_map/dot_general | solution.py:71
  115.3 0.0 reduce-scatter.5.cloned.1.call-update
  115.3 5.3 %select_reduce_fusion.1 = bf16[64,64]{1,0:T(8,128)(2,1)S(1)} fusion(f32[64,1024]{1,0:T(8,128)} %get-tuple-element.17, s32[64,64]{1,0:T(8,128)S(1)} %get-tuple-element.13, pred[64,64]{1,0:T(8,128)(4,1)S(1)} %get-tuple-element.14), kind=kLoop, calls=%fused_computation.2 | loop fusion | flops 16773120 | bytes 290816 | tf_op jit(solution)/shard_map/reduce_sum | solution.py:50
  120.7 0.0 collective-permute-start
  120.7 5.1 %collective-permute-done = bf16[64,64]{1,0:T(8,128)(2,1)S(1)} collective-permute-done((bf16[64,64]{1,0:T(8,128)(2,1)S(1)}, bf16[64,64]{1,0:T(8,128)(2,1)S(1)}, u32[]{:S(2)}, u32[]{:S(2)}) %collective-permute-start) | collective-permute-done | bytes 8224 | tf_op jit(solution)/shard_map/ppermute | solution.py:56
  125.8 0.0 collective-permute-start.1
  125.8 5.3 %collective-permute-done.1 = bf16[64,64]{1,0:T(8,128)(2,1)S(1)} collective-permute-done((bf16[64,64]{1,0:T(8,128)(2,1)S(1)}, bf16[64,64]{1,0:T(8,128)(2,1)S(1)}, u32[]{:S(2)}, u32[]{:S(2)}) %collective-permute-start.1) | collective-permute-done | bytes 8224 | tf_op jit(solution)/shard_map/ppermute | solution.py:56
  131.1 0.0 collective-permute-start.2
  131.1 5.1 %collective-permute-done.2 = bf16[64,64]{1,0:T(8,128)(2,1)S(1)} collective-permute-done((bf16[64,64]{1,0:T(8,128)(2,1)S(1)}, bf16[64,64]{1,0:T(8,128)(2,1)S(1)}, u32[]{:S(2)}, u32[]{:S(2)}) %collective-permute-start.2) | collective-permute-done | bytes 8224 | tf_op jit(solution)/shard_map/ppermute | solution.py:56
  136.3 0.0 collective-permute-start.3
  136.3 5.1 %collective-permute-done.3 = bf16[64,64]{1,0:T(8,128)(2,1)S(1)} collective-permute-done((bf16[64,64]{1,0:T(8,128)(2,1)S(1)}, bf16[64,64]{1,0:T(8,128)(2,1)S(1)}, u32[]{:S(2)}, u32[]{:S(2)}) %collective-permute-start.3) | collective-permute-done | bytes 8224 | tf_op jit(solution)/shard_map/ppermute | solution.py:56
  141.4 0.0 collective-permute-start.4
  141.4 5.2 %collective-permute-done.4 = bf16[64,64]{1,0:T(8,128)(2,1)S(1)} collective-permute-done((bf16[64,64]{1,0:T(8,128)(2,1)S(1)}, bf16[64,64]{1,0:T(8,128)(2,1)S(1)}, u32[]{:S(2)}, u32[]{:S(2)}) %collective-permute-start.4) | collective-permute-done | bytes 8224 | tf_op jit(solution)/shard_map/ppermute | solution.py:56
  146.6 0.0 collective-permute-start.5
  146.6 0.9 all_to_all.14
  147.5 1.7 copy.13
  149.2 4.8 %all-to-all-start = ((bf16[64,8,192]{2,0,1:T(8,128)(2,1)}), bf16[64,8,192]{2,0,1:T(8,128)(2,1)}, u32[]{:S(2)}, u32[]{:S(2)}) async-start(bf16[64,8,192]{2,0,1:T(8,128)(2,1)} %copy.13), calls=%async_computation.2 | async-start | bytes 524288 | tf_op jit(solution)/shard_map/all_to_all | solution.py:53
  154.1 0.0 all-reduce.6.cloned.1.call-start
  154.1 0.0 collective-permute-done.5
  154.1 0.5 collective-permute-start.6
  154.6 17.5 %all_gather.7 = s32[512,64]{1,0:T(8,128)S(1)} all-gather(s32[64,64]{1,0:T(8,128)S(1)} %get-tuple-element.13), channel_id=1, replica_groups=mesh['dp'=8,'leaf'=4] {'dp'}, dimensions={0}, use_global_device_ids=true | all-gather | bytes 147456 | tf_op jit(solution)/shard_map/all_gather | solution.py:60
  172.1 1.2 dynamic-slice
  174.0 0.0 collective-permute-done.6
  174.0 0.7 constant_dynamic-update-slice_fusion.15
  174.8 0.7 constant_dynamic-update-slice_fusion.7
  175.6 0.7 dynamic-slice_convert_fusion
  176.3 0.0 all-reduce.6.cloned.1.call-update
  176.4 28.3 %select_reduce_fusion = bf16[512,1024]{1,0:T(8,128)(2,1)} fusion(f32[512,64]{1,0:T(8,128)} %dynamic-slice_convert_fusion, s32[512,64]{1,0:T(8,128)S(1)} %all_gather.7), kind=kLoop, calls=%fused_computation | loop fusion | flops 100139008 | bytes 1310720 | tf_op jit(solution)/shard_map/reduce_sum | solution.py:14
  204.6 0.0 all-to-all-done
  204.6 2.6 %fusion.23 = f32[1024,192]{0,1:T(8,128)} fusion(bf16[512,1024]{1,0:T(8,128)(2,1)} %select_reduce_fusion, bf16[512,192]{1,0:T(8,128)(2,1)} %bitcast.2), kind=kOutput, calls=%fused_computation.72 | convolution fusion | flops 201326592 | bytes 2031616 | tf_op jit(solution)/shard_map/dot_general | solution.py:65
  207.2 26.9 %all-reduce.2 = (f32[1536]{0:T(1024)S(1)}, f32[1536]{0:T(1024)S(1)}) all-reduce(f32[1536]{0:T(1024)} %get-tuple-element.5, f32[1536]{0:T(1024)} %get-tuple-element.4), channel_id=4, replica_groups=mesh['dp'=8,'leaf'=4] {'dp'}, use_global_device_ids=true, to_apply=%region_8.9.clone | all-reduce | flops 3072 | bytes 24576
  234.1 0.1 dynamic-slice.1
  234.1 0.1 dynamic-slice.3
  234.2 9.8 %all-reduce.3 = (f32[192]{0:T(256)}, f32[192]{0:T(256)}) all-reduce(f32[192]{0:T(256)S(1)} %dynamic-slice.1, f32[192]{0:T(256)S(1)} %dynamic-slice.3), channel_id=1, replica_groups=mesh['dp'=8,'leaf'=4] {'leaf'}, use_global_device_ids=true, to_apply=%region_9.10 | all-reduce | flops 384 | bytes 3072 | tf_op jit(solution)/shard_map/psum | solution.py:81
  244.0 1.7 copy.30
  (19 shorter events, 0.1 us)
Async XLA Ops:
  7.2 49.8 %copy-start = (bf16[1024,1536]{1,0:T(8,128)(2,1)S(1)}, bf16[1024,1536]{1,0:T(8,128)(2,1)}, u32[]{:S(2)}) copy-start(bf16[1024,1536]{1,0:T(8,128)(2,1)} %param.11) | copy-start | bytes 9437188
  7.2 77.9 %reduce-scatter.3.cloned.1.call-start = ((), (), s32[]{:S(2)}) async-start(), calls=%async_computation.3 | async-start | bytes 491520 | tf_op jit(solution)/shard_map/reduce_scatter | solution.py:47
  30.1 15.5 %copy-start.4 = (s32[64]{0:T(128)S(1)}, s32[64]{0:T(128)}, u32[]{:S(2)}) copy-start(s32[64]{0:T(128)} %param.12) | copy-start | bytes 772
  30.1 17.3 %copy-start.1 = (s32[64,64]{1,0:T(8,128)S(1)}, s32[64,64]{1,0:T(8,128)}, u32[]{:S(2)}) copy-start(s32[64,64]{1,0:T(8,128)} %param.13) | copy-start | bytes 49156
  60.2 116.2 %reduce-scatter.5.cloned.1.call-start = ((), (), s32[]{:S(2)}) async-start(), calls=%async_computation.4 | async-start | bytes 2654208 | tf_op jit(solution)/shard_map/reduce_scatter | solution.py:77
  91.1 10.1 %copy-start.2 = (f32[1536]{0:T(1024)S(1)}, f32[1536]{0:T(1024)}, u32[]{:S(2)}) copy-start(f32[1536]{0:T(1024)} %param.10) | copy-start | bytes 18436
  91.2 10.1 %copy-start.3 = (f32[1536]{0:T(1024)S(1)}, f32[1536]{0:T(1024)}, u32[]{:S(2)}) copy-start(f32[1536]{0:T(1024)} %param.9) | copy-start | bytes 18436
  101.2 9.6 %copy-start.5 = (bf16[1600,384]{1,0:T(8,128)(2,1)S(1)}, bf16[1600,384]{1,0:T(8,128)(2,1)}, u32[]{:S(2)}) copy-start(bf16[1600,384]{1,0:T(8,128)(2,1)} %param.7) | copy-start | bytes 3686404
  120.7 5.1 %collective-permute-start = (bf16[64,64]{1,0:T(8,128)(2,1)S(1)}, bf16[64,64]{1,0:T(8,128)(2,1)S(1)}, u32[]{:S(2)}, u32[]{:S(2)}) collective-permute-start(bf16[64,64]{1,0:T(8,128)(2,1)S(1)} %select_reduce_fusion.1), channel_id=1, source_target_pairs={{0,4},{4,8},{8,12},{12,16},{16,20},{20,24},{24,28},{28,0},{1,5},{5... | collective-permute-start | bytes 24584 | tf_op jit(solution)/shard_map/ppermute | solution.py:56
  125.8 5.3 %collective-permute-start.1 = (bf16[64,64]{1,0:T(8,128)(2,1)S(1)}, bf16[64,64]{1,0:T(8,128)(2,1)S(1)}, u32[]{:S(2)}, u32[]{:S(2)}) collective-permute-start(bf16[64,64]{1,0:T(8,128)(2,1)S(1)} %collective-permute-done), channel_id=1, source_target_pairs={{0,4},{4,8},{8,12},{12,16},{16,20},{20,24},{24,28},{28,0},{1,5},{5... | collective-permute-start | bytes 24584 | tf_op jit(solution)/shard_map/ppermute | solution.py:56
  131.1 5.1 %collective-permute-start.2 = (bf16[64,64]{1,0:T(8,128)(2,1)S(1)}, bf16[64,64]{1,0:T(8,128)(2,1)S(1)}, u32[]{:S(2)}, u32[]{:S(2)}) collective-permute-start(bf16[64,64]{1,0:T(8,128)(2,1)S(1)} %collective-permute-done.1), channel_id=1, source_target_pairs={{0,4},{4,8},{8,12},{12,16},{16,20},{20,24},{24,28},{28,0},{1,5},{5... | collective-permute-start | bytes 24584 | tf_op jit(solution)/shard_map/ppermute | solution.py:56
  136.3 5.1 %collective-permute-start.3 = (bf16[64,64]{1,0:T(8,128)(2,1)S(1)}, bf16[64,64]{1,0:T(8,128)(2,1)S(1)}, u32[]{:S(2)}, u32[]{:S(2)}) collective-permute-start(bf16[64,64]{1,0:T(8,128)(2,1)S(1)} %collective-permute-done.2), channel_id=1, source_target_pairs={{0,4},{4,8},{8,12},{12,16},{16,20},{20,24},{24,28},{28,0},{1,5},{5... | collective-permute-start | bytes 24584 | tf_op jit(solution)/shard_map/ppermute | solution.py:56
  141.4 5.2 %collective-permute-start.4 = (bf16[64,64]{1,0:T(8,128)(2,1)S(1)}, bf16[64,64]{1,0:T(8,128)(2,1)S(1)}, u32[]{:S(2)}, u32[]{:S(2)}) collective-permute-start(bf16[64,64]{1,0:T(8,128)(2,1)S(1)} %collective-permute-done.3), channel_id=1, source_target_pairs={{0,4},{4,8},{8,12},{12,16},{16,20},{20,24},{24,28},{28,0},{1,5},{5... | collective-permute-start | bytes 24584 | tf_op jit(solution)/shard_map/ppermute | solution.py:56
  146.6 7.5 %collective-permute-start.5 = (bf16[64,64]{1,0:T(8,128)(2,1)S(1)}, bf16[64,64]{1,0:T(8,128)(2,1)S(1)}, u32[]{:S(2)}, u32[]{:S(2)}) collective-permute-start(bf16[64,64]{1,0:T(8,128)(2,1)S(1)} %collective-permute-done.4), channel_id=1, source_target_pairs={{0,4},{4,8},{8,12},{12,16},{16,20},{20,24},{24,28},{28,0},{1,5},{5... | collective-permute-start | bytes 24584 | tf_op jit(solution)/shard_map/ppermute | solution.py:56
  149.2 55.4 %all-to-all-start = ((bf16[64,8,192]{2,0,1:T(8,128)(2,1)}), bf16[64,8,192]{2,0,1:T(8,128)(2,1)}, u32[]{:S(2)}, u32[]{:S(2)}) async-start(bf16[64,8,192]{2,0,1:T(8,128)(2,1)} %copy.13), calls=%async_computation.2 | async-start | bytes 524288 | tf_op jit(solution)/shard_map/all_to_all | solution.py:53
  154.1 89.9 %all-reduce.6.cloned.1.call-start = ((), (), s32[]{:S(2)}) async-start(), calls=%async_computation.5 | async-start | bytes 589824 | tf_op jit(solution)/shard_map/psum | solution.py:81
  154.1 19.9 %collective-permute-start.6 = (bf16[64,64]{1,0:T(8,128)(2,1)S(1)}, bf16[64,64]{1,0:T(8,128)(2,1)}, u32[]{:S(2)}, u32[]{:S(2)}) collective-permute-start(bf16[64,64]{1,0:T(8,128)(2,1)S(1)} %collective-permute-done.5), channel_id=1, source_target_pairs={{0,4},{4,8},{8,12},{12,16},{16,20},{20,24},{24,28},{28,0},{1,5},{5... | collective-permute-start | bytes 24584 | tf_op jit(solution)/shard_map/ppermute | solution.py:56
Sparse Core Ops, SparseCore 0:
  60.3 24.7 reduce-scatter.2
  115.5 37.1 reduce-scatter.4
  176.5 41.4 all-reduce.5
